TPU v7x, 128 devices: a whole 4x4x4 slice. The times are simulated.
128 devices in a mesh: tile: 32 (over x_lo, y, z), src: 4 (over x_hi, core).
Axes of the slice: x: 4 (x_hi: 2, x_lo: 2; x = x_hi * 2 + x_lo), y: 4, z: 4, core: 2. Of those that a mesh axis runs over, the one named last changes fastest.
Arguments:
- tile_tokens: bfloat16 [32768, 2048], P(('tile', 'src')), may hold values from -6 to 6
- norm_gain: float32 [2048], replicated, may hold values from 0.25 to 2.5
- up_weight: bfloat16 [2048, 2816], P('tile'), may hold values from -0.125 to 0.125
- down_weight: bfloat16 [2816, 2048], P('tile'), may hold values from -0.109375 to 0.109375
- head_weight: bfloat16 [2048, 768], P(None, 'src'), may hold values from -0.125 to 0.125
- source_index: int32 [128, 2], replicated, may hold values from 0 to 96, as said below
- source_cutoff: int32 [128], replicated, may hold values from 8 to 16
- source_weight: float32 [128], replicated, may hold values from 0.3 to 3
Outputs:
- intensity: float32 [128, 4096], P(('tile', 'src'))
Inputs may be any that keep to these rules, and one draw needn't show every extreme that they name: `source_index`: in each aligned group of 4 source points the first has the least value of the group in both coordinates, the second lies exactly 32 beyond it in both, and every other lies within 32 of the first in both.
All inputs are finite; a program needn't handle non-finite values.
Results may differ from a plain program's by a relative error of at most 0.0007.
Values may be sent and summed in bfloat16 or wider, within the bound.
No kernel may reach another device: no remote copies, remote signals or barrier semaphores. Data moves between devices by JAX's collectives and lax.ppermute only.
A program may use at most 128 MiB of HBM per device.

v0:
```python
import math
import jax
import jax.numpy as jnp
from jax import lax
from jax.sharding import PartitionSpec as P

GRID = 16
SUB = 8
W = 32
REG = 64
PIX = 64
SRC_DEV = 4
PATCH = 256
ORD = 128
f32 = jnp.float32
bf16 = jnp.bfloat16


def split_bf16(x):
    hi = lax.reduce_precision(x, exponent_bits=8, mantissa_bits=7)
    lo = x - hi
    return (hi.astype(bf16), lo.astype(bf16))


def phase_tables():
    turn = 2.0 * math.pi / PIX
    v = jnp.arange(ORD, dtype=jnp.int32)
    y = jnp.arange(PIX, dtype=jnp.int32)
    ang = jnp.mod(v[:, None] * y[None, :], PIX).astype(f32) * turn
    cv, sv = (jnp.cos(ang), jnp.sin(ang))
    t1 = jnp.stack([jnp.concatenate([cv, sv], 1), jnp.concatenate([-sv, cv], 1)], 0)
    i = jnp.arange(W, dtype=jnp.int32)
    x = jnp.arange(PIX, dtype=jnp.int32)
    ang2 = jnp.mod(x[:, None] * i[None, :], PIX).astype(f32) * turn
    ca, sa = (jnp.cos(ang2), jnp.sin(ang2))
    t2 = jnp.stack([jnp.stack([ca, -sa], 1), jnp.stack([sa, ca], 1)], 0)
    return (t1, t2)


def imaging(spec, source_index, source_cutoff, source_weight):
    T = spec.shape[0]
    S = source_index.shape[0]
    x0 = jnp.clip(source_index[:, 0], 0, ORD - W)
    y0 = jnp.clip(source_index[:, 1], 0, ORD - W)
    rows = x0[:, None] + jnp.arange(W, dtype=jnp.int32)[None, :]
    pick = (rows[:, :, None] == jnp.arange(ORD, dtype=jnp.int32)[None, None, :]).astype(bf16)
    spec_rows = spec.reshape(T, 6, 2, ORD, ORD)
    strips = jnp.einsum("siu,tkpuv->sitkpv", pick, spec_rows, preferred_element_type=f32).astype(
        bf16
    )
    i = jnp.arange(W, dtype=jnp.int32)
    j = jnp.arange(ORD, dtype=jnp.int32)[None, :] - y0[:, None]
    dist = (i[None, :, None] - W // 2) ** 2 + (j[:, None, :] - W // 2) ** 2
    keep = (
        (dist <= (source_cutoff * source_cutoff)[:, None, None])
        & (j[:, None, :] >= 0)
        & (j[:, None, :] < W)
    )
    masked = jnp.where(keep[:, :, None, None, None, :], strips, jnp.zeros((), bf16))
    t1, t2 = phase_tables()
    half = jnp.einsum("sitkpv,pvn->sitkn", masked.astype(f32), t1, precision=lax.Precision.HIGH)
    half = half.reshape(S, W, T, 6, 2, PIX)
    field = jnp.einsum("cxqi,sitkqy->tskcxy", t2, half, precision=lax.Precision.HIGH)
    power = jnp.sum(field * field * source_weight[None, :, None, None, None, None], axis=(1, 2, 3))
    return power.reshape(T, PIX * PIX) * (1.0 / (6.0 * W * W * S))


def local(
    tile_tokens,
    norm_gain,
    up_weight,
    down_weight,
    head_weight,
    source_index,
    source_cutoff,
    source_weight,
):
    token_count, d_model = tile_tokens.shape
    n_tile = lax.axis_size("tile")
    n_src = lax.axis_size("src")
    me = lax.axis_index("src")
    half = me % 2
    up_rows, ff = up_weight.shape
    down_rows = down_weight.shape[0]
    up_half, down_half = (up_rows // 2, down_rows // 2)
    depth = -(-(up_half + down_half) // 16) * 16
    width = max(ff, d_model)
    up_part = lax.dynamic_slice_in_dim(up_weight, half * up_half, up_half, 0)
    down_part = lax.dynamic_slice_in_dim(down_weight, half * down_half, down_half, 0)
    packed = jnp.concatenate(
        [
            jnp.pad(up_part, ((0, 0), (0, width - ff))),
            jnp.pad(down_part, ((0, depth - up_half - down_half), (0, width - d_model))),
        ],
        0,
    )
    gathered = lax.all_gather(packed, "tile", axis=0, tiled=True)
    sibling = lax.ppermute(gathered, "src", [(s, s ^ 1) for s in range(n_src)])
    head_parts = [head_weight] + [
        lax.ppermute(head_weight, "src", [(s, s ^ k) for s in range(n_src)])
        for k in range(1, n_src)
    ]
    residual = tile_tokens.astype(jnp.float32)
    mean_square = jnp.mean(residual * residual, axis=1, keepdims=True)
    normed = (residual * lax.rsqrt(mean_square + 1e-05) * norm_gain).astype(jnp.bfloat16)

    def spread(x, rows, start):
        view = x.reshape(x.shape[0], n_tile, 2, rows // 2)
        pad = ((0, 0), (0, 0), (start, depth - start - rows // 2))
        mine = jnp.pad(lax.dynamic_index_in_dim(view, half, 2, keepdims=False), pad)
        other = jnp.pad(lax.dynamic_index_in_dim(view, 1 - half, 2, keepdims=False), pad)
        return (mine.reshape(x.shape[0], -1), other.reshape(x.shape[0], -1))

    normed_mine, normed_other = spread(normed, up_rows, 0)
    pre_act = jnp.dot(normed_mine, gathered, preferred_element_type=jnp.float32) + jnp.dot(
        normed_other, sibling, preferred_element_type=jnp.float32
    )
    hidden = jax.nn.gelu(pre_act[:, :ff]).astype(jnp.bfloat16)
    hidden_mine, hidden_other = spread(hidden, down_rows, up_half)
    branch_out = jnp.dot(hidden_mine, gathered, preferred_element_type=jnp.float32) + jnp.dot(
        hidden_other, sibling, preferred_element_type=jnp.float32
    )
    branch_out = branch_out[:, :d_model]
    mixed = (residual + branch_out).astype(jnp.bfloat16)
    parts = jnp.stack(head_parts, 0)
    coeff_parts = jnp.einsum(
        "tk,pkc->ptc", mixed, parts, preferred_element_type=jnp.float32
    ).astype(jnp.bfloat16)
    order = me ^ jnp.arange(n_src, dtype=jnp.int32)
    coeffs = jnp.take(coeff_parts, order, axis=0).transpose(1, 0, 2).reshape(token_count, -1)
    tile_count = token_count // PATCH
    spectra = (
        coeffs.reshape(tile_count, GRID, GRID, 12, SUB, SUB)
        .transpose(0, 3, 1, 4, 2, 5)
        .reshape(tile_count, 12, ORD, ORD)
    )
    return imaging(spectra, source_index, source_cutoff, source_weight)


def solution(mesh):
    return jax.shard_map(
        local,
        mesh=mesh,
        in_specs=(
            P(("tile", "src"), None),
            P(),
            P("tile", None),
            P("tile", None),
            P(None, "src"),
            P(),
            P(),
            P(),
        ),
        out_specs=P(("tile", "src"), None),
        check_vma=False,
    )
```

profile of v0, /device:TPU:1, one launch (start us, length us, event | category | flops | bytes accessed | tf_op | source)
XLA Modules:
  0.0 335.5 jit_solution(13254922369213393428)
XLA Ops:
  6.6 1.0 copy-done
  7.6 0.9 constant_dynamic-slice_fusion.1
  8.5 0.8 fusion.45
  9.3 170.6 %all-gather.2.cloned.1.call-done = bf16[2560,2816]{1,0:T(8,128)(2,1)} async-done(((bf16[80,2816]{1,0:T(8,128)(2,1)}), bf16[2560,2816]{1,0:T(8,128)(2,1)}) %all-gather.2.cloned.1.call-update) | async-done | bytes 14417936 | tf_op jit(solution)/shard_map/all_gather | solution.py:97
  179.9 15.1 %collective-permute-start.3 = (bf16[2560,2816]{1,0:T(8,128)(2,1)}, bf16[2560,2816]{1,0:T(8,128)(2,1)}, u32[]{:S(2)}, u32[]{:S(2)}) collective-permute-start(bf16[2560,2816]{1,0:T(8,128)(2,1)} %all-gather.2.cloned.1.call-done), channel_id=1, source_target_pairs={{0,1},{1,0},{2,3},{3,2},{4,5},{5,4},{6,7},{7,6},{8,9},{9,8},{10,11... | collective-permute-start | bytes 43253768 | tf_op jit(solution)/shard_map/ppermute | solution.py:98
  195.0 3.1 collective-permute-start.1
  198.1 0.5 collective-permute-start.2
  198.6 1.5 fusion.26
  200.2 0.3 fusion.28
  200.5 0.5 copy.27
  201.3 0.4 copy-done.9
  202.1 0.1 fusion.61
  202.2 0.6 maximum_bitcast_fusion.4
  203.2 2.4 fusion.31
  205.6 7.6 %fusion.72 = f32[256,2816]{1,0:T(8,128)S(1)} fusion(bf16[256,2560]{0,1:T(8,128)(2,1)S(1)} %bitcast.100, bf16[2560,2816]{1,0:T(8,128)(2,1)} %all-gather.2.cloned.1.call-done), kind=kOutput, calls=%fused_computation.107 | convolution fusion | flops 3690987520 | bytes 18612224 | tf_op jit(solution)/shard_map/dot_general | solution.py:115
  213.2 3.5 %collective-permute-done.3 = bf16[2560,2816]{1,0:T(8,128)(2,1)} collective-permute-done((bf16[2560,2816]{1,0:T(8,128)(2,1)}, bf16[2560,2816]{1,0:T(8,128)(2,1)}, u32[]{:S(2)}, u32[]{:S(2)}) %collective-permute-start.3) | collective-permute-done | bytes 14417952 | tf_op jit(solution)/shard_map/ppermute | solution.py:98
  216.7 9.9 %fusion.25 = bf16[256,2816]{1,0:T(8,128)(2,1)S(1)} fusion(f32[256,2816]{1,0:T(8,128)S(1)} %fusion.72, bf16[256,2560]{0,1:T(8,128)(2,1)S(1)} %bitcast.104, bf16[2560,2816]{1,0:T(8,128)(2,1)} %collective-permute-done.3), kind=kOutput, calls=%fused_computation.31 | convolution fusion | flops 3698196480 | bytes 20054016 | tf_op jit(solution)/shard_map/dot_general | solution.py:115
  226.7 0.7 copy.28
  227.4 0.3 reshape.262
  228.0 7.6 %fusion.73 = f32[256,2816]{1,0:T(8,128)S(1)} fusion(bf16[256,2560]{0,1:T(8,128)(2,1)S(1)} %bitcast.101, bf16[2560,2816]{1,0:T(8,128)(2,1)} %all-gather.2.cloned.1.call-done), kind=kOutput, calls=%fused_computation.108 | convolution fusion | flops 3690987520 | bytes 18612224 | tf_op jit(solution)/shard_map/dot_general | solution.py:120
  235.7 7.9 %fusion.74 = f32[256,2816]{1,0:T(8,128)S(1)} fusion(bf16[256,2560]{0,1:T(8,128)(2,1)S(1)} %bitcast.102, bf16[2560,2816]{1,0:T(8,128)(2,1)} %collective-permute-done.3), kind=kOutput, calls=%fused_computation.109 | convolution fusion | flops 3690987520 | bytes 18612224 | tf_op jit(solution)/shard_map/dot_general | solution.py:120
  243.7 2.7 fusion.38
  246.3 0.6 gather_fusion
  246.9 0.9 select_bitcast_fusion
  247.8 3.5 %reshape_reshape.4 = bf16[1,16,16,12,8,8]{2,1,5,4,3,0:T(8,128)(2,1)S(1)} reshape(bf16[256,4,192]{0,2,1:T(8,128)(2,1)} %select_bitcast_fusion) | data formatting | bytes 786432 | tf_op jit(solution)/shard_map/reshape;reshape | solution.py:133
  251.3 5.3 %copy.33 = bf16[1,16,16,12,8,8]{5,2,4,1,3,0:T(8,128)(2,1)} copy(bf16[1,16,16,12,8,8]{2,1,5,4,3,0:T(8,128)(2,1)S(1)} %reshape_reshape.4) | data formatting | bytes 786432 | tf_op jit(solution)/shard_map/reshape;reshape | solution.py:133
  256.6 8.2 %reshape.276 = bf16[6,2,128,128,1]{3,2,1,0,4:T(8,128)(2,1)S(1)} reshape(bf16[1,12,16,8,16,8]{5,4,3,2,1,0:T(8,128)(2,1)} %bitcast.99) | data formatting | bytes 786432 | tf_op jit(solution)/shard_map/reshape.2
  264.8 6.5 %fusion.33 = bf16[128,32,6,2,128]{4,1,3,2,0:T(8,128)(2,1)} fusion(bf16[6,2,128,128,1]{3,2,1,0,4:T(8,128)(2,1)S(1)} %reshape.276, s32[128,32]{1,0:T(8,128)S(1)} %iota_add_fusion), kind=kOutput, calls=%fused_computation.42 | convolution fusion | flops 1611137024 | bytes 12992512 | tf_op jit(solution)/shard_map/siu,tkpuv->sitkpv/dot_general | solution.py:48
  271.3 14.6 %fusion.6 = f32[128,32,6,2,64,1]{4,1,3,2,0,5:T(8,128)} fusion(f32[2,64,2,128,1,1]{3,1,0,2,5,4:T(8,128)S(1)} %bitcast.105, bf16[128,32,6,2,128]{4,1,3,2,0:T(8,128)(2,1)} %fusion.33, pred[128,32,128]{2,1,0:T(8,128)(4,1)S(1)} %copy-done.2), kind=kOutput, calls=%fused_computation.9 | convolution fusion | flops 4838129664 | bytes 25821184 | tf_op jit(solution)/shard_map/sitkpv,pvn->sitkn/dot_general | solution.py:61
  286.0 22.9 %copy.42 = f32[128,32,6,2,64,1]{0,1,3,5,4,2:T(8,128)} copy(f32[128,32,6,2,64,1]{4,1,3,2,0,5:T(8,128)} %fusion.6) | data formatting | bytes 25165824 | tf_op jit(solution)/shard_map/sitkpv,pvn->sitkn/dot_general | solution.py:61
  308.8 19.0 %fusion = f32[64,64]{1,0:T(8,128)S(1)} fusion(f32[128]{0:T(128)S(1)} %copy-done.10, f32[128,32,6,2,64,1]{0,1,3,5,4,2:T(8,128)} %copy.42, f32[1,64,2,32]{1,3,2,0:T(8,128)S(1)} %copy-done.5, f32[1,64,2,32]{1,3,2,0:T(8,128)S(1)} %get-tuple-element.11), kind=kOutput, calls=%fused_computation.2 | convolution fusion | flops 2434797568 | bytes 12632576 | tf_op jit(solution)/shard_map/cxqi,sitkqy->tskcxy/dot_general | solution.py:63
  328.0 0.7 mul.233
  (50 shorter events, 1.4 us)
Async XLA Ops:
  6.5 1.0 copy-start
  6.5 193.6 %copy-start.3 = (bf16[256,2048]{1,0:T(8,128)(2,1)S(1)}, bf16[256,2048]{1,0:T(8,128)(2,1)}, u32[]{:S(2)}) copy-start(bf16[256,2048]{1,0:T(8,128)(2,1)} %param.8) | copy-start | bytes 3145732
  6.5 193.6 %copy-start.6 = (f32[2048]{0:T(1024)S(1)}, f32[2048]{0:T(1024)}, u32[]{:S(2)}) copy-start(f32[2048]{0:T(1024)} %param.9) | copy-start | bytes 24580
  6.5 173.4 %all-gather.2.cloned.1.call-start = ((), (), s32[]{:S(2)}) async-start(), calls=%async_computation | async-start | bytes 14868480 | tf_op jit(solution)/shard_map/all_gather | solution.py:97
  179.9 36.8 %collective-permute-start.3 = (bf16[2560,2816]{1,0:T(8,128)(2,1)}, bf16[2560,2816]{1,0:T(8,128)(2,1)}, u32[]{:S(2)}, u32[]{:S(2)}) collective-permute-start(bf16[2560,2816]{1,0:T(8,128)(2,1)} %all-gather.2.cloned.1.call-done), channel_id=1, source_target_pairs={{0,1},{1,0},{2,3},{3,2},{4,5},{5,4},{6,7},{7,6},{8,9},{9,8},{10,11... | collective-permute-start | bytes 43253768 | tf_op jit(solution)/shard_map/ppermute | solution.py:98
  195.0 48.6 %collective-permute-start = (bf16[2048,192]{0,1:T(8,128)(2,1)}, bf16[2048,192]{0,1:T(8,128)(2,1)}, u32[]{:S(2)}, u32[]{:S(2)}) collective-permute-start(bf16[2048,192]{0,1:T(8,128)(2,1)} %param.12), channel_id=1, source_target_pairs={{0,1},{1,0},{2,3},{3,2},{4,5},{5,4},{6,7},{7,6},{8,9},{9,8},{10,11... | collective-permute-start | bytes 2359304 | tf_op jit(solution)/shard_map/ppermute | solution.py:100
  195.0 48.6 %collective-permute-start.1 = (bf16[2048,192]{0,1:T(8,128)(2,1)}, bf16[2048,192]{0,1:T(8,128)(2,1)}, u32[]{:S(2)}, u32[]{:S(2)}) collective-permute-start(bf16[2048,192]{0,1:T(8,128)(2,1)} %param.12), channel_id=1, source_target_pairs={{0,2},{1,3},{2,0},{3,1},{4,6},{5,7},{6,4},{7,5},{8,10},{9,11},{10,... | collective-permute-start | bytes 2359304 | tf_op jit(solution)/shard_map/ppermute | solution.py:100
  198.1 45.5 %collective-permute-start.2 = (bf16[2048,192]{0,1:T(8,128)(2,1)}, bf16[2048,192]{0,1:T(8,128)(2,1)}, u32[]{:S(2)}, u32[]{:S(2)}) collective-permute-start(bf16[2048,192]{0,1:T(8,128)(2,1)} %param.12), channel_id=1, source_target_pairs={{0,3},{1,2},{2,1},{3,0},{4,7},{5,6},{6,5},{7,4},{8,11},{9,10},{10,... | collective-permute-start | bytes 2359304 | tf_op jit(solution)/shard_map/ppermute | solution.py:100
  201.0 0.7 copy-start.9
  201.0 1.8 copy-start.7
  235.6 8.0 %copy-start.4 = (bf16[256,2048]{1,0:T(8,128)(2,1)S(1)}, bf16[256,2048]{1,0:T(8,128)(2,1)}, u32[]{:S(2)}) copy-start(bf16[256,2048]{1,0:T(8,128)(2,1)} %param.8) | copy-start | bytes 3145732
  235.7 8.0 %copy-start.8 = (bf16[2048,192]{0,1:T(8,128)(2,1)S(1)}, bf16[2048,192]{0,1:T(8,128)(2,1)}, u32[]{:S(2)}) copy-start(bf16[2048,192]{0,1:T(8,128)(2,1)} %param.12) | copy-start | bytes 2359300
  264.8 6.5 %copy-start.2 = (pred[128,32,128]{2,1,0:T(8,128)(4,1)S(1)}, pred[128,32,128]{2,1,0:T(8,128)(4,1)}, u32[]{:S(2)}) copy-start(pred[128,32,128]{2,1,0:T(8,128)(4,1)} %fusion.31) | copy-start | bytes 1572868
  285.9 22.9 %copy-start.5 = (f32[1,64,2,32]{1,3,2,0:T(8,128)S(1)}, f32[1,64,2,32]{1,3,2,0:T(8,128)}, u32[]{:S(2)}) copy-start(f32[1,64,2,32]{1,3,2,0:T(8,128)} %get-tuple-element.12) | copy-start | bytes 49156
  285.9 22.9 %copy-start.10 = (f32[128]{0:T(128)S(1)}, f32[128]{0:T(128)}, u32[]{:S(2)}) copy-start(f32[128]{0:T(128)} %param.15) | copy-start | bytes 1540
  308.8 19.8 %copy-start.1 = (bf16[88,2048]{1,0:T(8,128)(2,1)S(1)}, bf16[88,2048]{1,0:T(8,128)(2,1)}, u32[]{:S(2)}) copy-start(bf16[88,2048]{1,0:T(8,128)(2,1)} %param.11) | copy-start | bytes 1081348
Sparse Core Ops, SparseCore 0:
  9.5 170.4 all-gather.1
where the time goes:
time: 336 us
  waiting for transfers between devices  174 us (52%)
  matrix products  75.9 us (23%)
  local copies, waits for them, and re-layouts  45.7 us (14%)
  starting transfers between devices  18.7 us (6%)
  between operations  13.8 us (4%)
  other arithmetic  7.29 us (2%)
    all_gather x1, waiting for transfers between devices, local(): gathered = lax.all_gather(packed, 'tile', axis=0, tiled=True)  171 us
    dot_general x1, local copies, waits for them, and re-layouts, imaging(): jnp.einsum('sitkpv,pvn->sitkn', masked.astype(f32), t1, precision=lax.Pre...  22.9 us
    dot_general x1, matrix products, imaging(): jnp.einsum('cxqi,sitkqy->tskcxy', t2, half, precision=lax.Precision.HIGH)  19 us
    ppermute x1, starting transfers between devices, local(): sibling = lax.ppermute(gathered, 'src', [(s, s ^ 1) for s in range(n_src)])  15.1 us
    dot_general x1, matrix products, imaging(): jnp.einsum('sitkpv,pvn->sitkn', masked.astype(f32), t1, precision=lax.Pre...  14.6 us
    dot_general x1, matrix products, local(): jnp.dot(normed_other, sibling, preferred_element_type=jnp.float32)  9.91 us
    another operation x2, local copies, waits for them, and re-layouts, local(): coeffs.reshape(tile_count, GRID, GRID, 12, SUB, SUB)  8.8 us
    another operation x1, local copies, waits for them, and re-layouts  8.2 us
  transfers between devices with their start and end apart: 5, of which 2 were waited for; matrix products, arithmetic and copies ran while one was open for 12% of the time, Pallas kernels for 0%

commit v1 on v0

--- a/solution.py
+++ b/solution.py
@@ -14,6 +14,13 @@
 ORD = 128
 f32 = jnp.float32
 bf16 = jnp.bfloat16
+
+
+def all_by_exchange(shard, axis, dim):
+    devices = lax.axis_size(axis)
+    shards = jnp.stack([shard for _ in range(devices)])
+    shards = lax.all_to_all(shards, axis, split_axis=0, concat_axis=0)
+    return jnp.concatenate(shards, axis=dim)
 
 
 def split_bf16(x):
@@ -94,7 +101,7 @@
         ],
         0,
     )
-    gathered = lax.all_gather(packed, "tile", axis=0, tiled=True)
+    gathered = all_by_exchange(packed, "tile", 0)
     sibling = lax.ppermute(gathered, "src", [(s, s ^ 1) for s in range(n_src)])
     head_parts = [head_weight] + [
         lax.ppermute(head_weight, "src", [(s, s ^ k) for s in range(n_src)])

time: 336 us -> 320 us (0.952)
  blocking collectives: 0 us -> 173 us
  waiting for transfers between devices: 174 us -> 5.23 us
  between operations: 13.8 us -> 0.36 us
  starting transfers between devices: 18.7 us -> 5.38 us
  local copies, waits for them, and re-layouts: 45.7 us -> 51 us
    all_to_all x0 -> x1, blocking collectives: none -> 173 us  [all_by_exchange(): shards = lax.all_to_all(shards, axis, split_axis=0, concat_axis=0)]
    all_gather x1 -> x0, waiting for transfers between devices: 171 us -> none  [local(): gathered = lax.all_gather(packed, 'tile', axis=0, tiled=True)]
    ppermute x1, starting transfers between devices: 15.1 us -> 1.74 us  [local(): sibling = lax.ppermute(gathered, 'src', [(s, s ^ 1) for s in range(n_src)])]
    another operation x1 -> x2, local copies, waits for them, and re-layouts: 8.2 us -> 14.2 us
  transfers between devices with their start and end apart: 5 -> 4, of which waited for: 2 -> 1; matrix products, arithmetic and copies ran while one was open for 12% -> 13% of each run, Pallas kernels for 0% -> 0%
where the time goes in v1:
time: 320 us; the launch traced here: 319 us
  blocking collectives  173 us (54%)
  matrix products  78.7 us (25%)
  local copies, waits for them, and re-layouts  51 us (16%)
  starting transfers between devices  5.38 us (2%)
  other arithmetic  5.28 us (2%)
  waiting for transfers between devices  5.23 us (2%)
    all_to_all x1, blocking collectives, all_by_exchange(): shards = lax.all_to_all(shards, axis, split_axis=0, concat_axis=0)  173 us
    dot_general x1, local copies, waits for them, and re-layouts, imaging(): jnp.einsum('sitkpv,pvn->sitkn', masked.astype(f32), t1, precision=lax.Pre...  22.7 us
    dot_general x1, matrix products, imaging(): jnp.einsum('cxqi,sitkqy->tskcxy', t2, half, precision=lax.Precision.HIGH)  19 us
    dot_general x1, matrix products, imaging(): jnp.einsum('sitkpv,pvn->sitkn', masked.astype(f32), t1, precision=lax.Pre...  14.6 us
    dot_general x1, matrix products, local(): jnp.dot(hidden_mine, gathered, preferred_element_type=jnp.float32)  10.5 us
    dot_general x1, matrix products, local(): jnp.dot(normed_other, sibling, preferred_element_type=jnp.float32)  9.91 us
    another operation x2, local copies, waits for them, and re-layouts, local(): coeffs.reshape(tile_count, GRID, GRID, 12, SUB, SUB)  8.8 us
    another operation x1, local copies, waits for them, and re-layouts  8.2 us
  transfers between devices with their start and end apart: 4, of which 1 were waited for; matrix products, arithmetic and copies ran while one was open for 13% of the time, Pallas kernels for 0%

profile of v1, /device:TPU:1, one launch (start us, length us, event | category | flops | bytes accessed | tf_op | source)
XLA Modules:
  0.0 319.2 jit_solution(6835644848222443638)
XLA Ops:
  0.0 1.0 copy-done
  1.0 0.9 constant_dynamic-slice_fusion.2
  2.0 6.0 %stack.33 = bf16[32,80,2816]{2,1,0:T(8,128)(2,1)} broadcast(bf16[80,2816]{1,0:T(8,128)(2,1)S(1)} %fusion.53), dimensions={1,2} | broadcast | bytes 14868480 | tf_op jit(solution)/shard_map/stack | solution.py:21
  8.0 173.2 %all_to_all.5 = bf16[32,80,2816]{2,1,0:T(8,128)(2,1)} all-to-all(bf16[32,80,2816]{2,1,0:T(8,128)(2,1)} %stack.33), channel_id=1, replica_groups=mesh['tile'=32,'src'=4] {'tile'}, dimensions={0} | all-to-all | bytes 28835840 | tf_op jit(solution)/shard_map/all_to_all | solution.py:22
  181.3 1.7 collective-permute-start.3
  183.0 2.5 collective-permute-start.1
  185.5 1.2 collective-permute-start.2
  186.7 0.3 fusion.31
  187.0 0.3 fusion.33
  187.3 0.5 copy.27
  188.2 0.1 fusion.72
  188.4 0.1 fusion.69
  188.6 0.6 maximum_bitcast_fusion.4
  189.5 2.4 fusion.36
  191.9 7.6 %convolution_bitcast_fusion = f32[256,2816]{1,0:T(8,128)S(1)} fusion(bf16[32,80,2816]{2,1,0:T(8,128)(2,1)} %all_to_all.5, bf16[256,32,32]{0,2,1:T(8,128)(2,1)S(1)} %get-tuple-element.8), kind=kOutput, calls=%fused_computation.14 | convolution fusion | flops 3690987520 | bytes 17825792 | tf_op jit(solution)/shard_map/dot_general | solution.py:122
  199.5 5.2 %collective-permute-done.3 = bf16[2560,2816]{1,0:T(8,128)(2,1)} collective-permute-done((bf16[2560,2816]{1,0:T(8,128)(2,1)}, bf16[2560,2816]{1,0:T(8,128)(2,1)}, u32[]{:S(2)}, u32[]{:S(2)}) %collective-permute-start.3) | collective-permute-done | bytes 14417952 | tf_op jit(solution)/shard_map/ppermute | solution.py:105
  204.8 9.9 %fusion.30 = bf16[256,2816]{1,0:T(8,128)(2,1)S(1)} fusion(f32[256,2816]{1,0:T(8,128)S(1)} %convolution_bitcast_fusion, bf16[256,2560]{0,1:T(8,128)(2,1)S(1)} %bitcast.102, bf16[2560,2816]{1,0:T(8,128)(2,1)} %collective-permute-done.3), kind=kOutput, calls=%fused_computation.35 | convolution fusion | flops 3698196480 | bytes 20054016 | tf_op jit(solution)/shard_map/dot_general | solution.py:122
  214.7 0.7 copy.28
  215.4 0.3 reshape.263
  215.9 7.6 %fusion.81 = f32[256,2816]{1,0:T(8,128)S(1)} fusion(bf16[256,2560]{0,1:T(8,128)(2,1)S(1)} %bitcast.100, bf16[2560,2816]{1,0:T(8,128)(2,1)} %collective-permute-done.3), kind=kOutput, calls=%fused_computation.115 | convolution fusion | flops 3690987520 | bytes 18612224 | tf_op jit(solution)/shard_map/dot_general | solution.py:127
  223.6 10.5 %fusion.12 = f32[256,2816]{1,0:T(8,128)S(1)} fusion(bf16[32,80,2816]{2,1,0:T(8,128)(2,1)} %all_to_all.5, bf16[256,32,1,44]{0,3,2,1:T(8,128)(2,1)S(1)} %get-tuple-element.5), kind=kOutput, calls=%fused_computation.15 | convolution fusion | flops 2030043136 | bytes 18022400 | tf_op jit(solution)/shard_map/dot_general | solution.py:127
  234.1 3.0 fusion.44
  237.1 0.6 gather_fusion
  237.6 0.8 select_bitcast_fusion
  238.5 3.5 %reshape_reshape.4 = bf16[1,16,16,12,8,8]{2,1,5,4,3,0:T(8,128)(2,1)S(1)} reshape(bf16[256,4,192]{0,2,1:T(8,128)(2,1)} %select_bitcast_fusion) | data formatting | bytes 786432 | tf_op jit(solution)/shard_map/reshape;reshape | solution.py:140
  242.0 5.3 %copy.33 = bf16[1,16,16,12,8,8]{5,2,4,1,3,0:T(8,128)(2,1)} copy(bf16[1,16,16,12,8,8]{2,1,5,4,3,0:T(8,128)(2,1)S(1)} %reshape_reshape.4) | data formatting | bytes 786432 | tf_op jit(solution)/shard_map/reshape;reshape | solution.py:140
  247.3 8.2 %reshape.278 = bf16[6,2,128,128,1]{3,2,1,0,4:T(8,128)(2,1)S(1)} reshape(bf16[1,12,16,8,16,8]{5,4,3,2,1,0:T(8,128)(2,1)} %bitcast.99) | data formatting | bytes 786432 | tf_op jit(solution)/shard_map/reshape.3
  255.5 6.5 %fusion.38 = bf16[128,32,6,2,128]{4,1,3,2,0:T(8,128)(2,1)} fusion(bf16[6,2,128,128,1]{3,2,1,0,4:T(8,128)(2,1)S(1)} %reshape.278, s32[128,32]{1,0:T(8,128)S(1)} %iota_add_fusion), kind=kOutput, calls=%fused_computation.46 | convolution fusion | flops 1611137024 | bytes 12992512 | tf_op jit(solution)/shard_map/siu,tkpuv->sitkpv/dot_general | solution.py:55
  262.0 14.6 %fusion.8 = f32[128,32,6,2,64,1]{4,1,3,2,0,5:T(8,128)} fusion(f32[2,64,2,128,1,1]{3,1,0,2,5,4:T(8,128)S(1)} %bitcast.103, bf16[128,32,6,2,128]{4,1,3,2,0:T(8,128)(2,1)} %fusion.38, pred[128,32,128]{2,1,0:T(8,128)(4,1)S(1)} %copy-done.2), kind=kOutput, calls=%fused_computation.11 | convolution fusion | flops 4838129664 | bytes 25821184 | tf_op jit(solution)/shard_map/sitkpv,pvn->sitkn/dot_general | solution.py:68
  276.6 22.7 %copy.42 = f32[128,32,6,2,64,1]{0,1,3,5,4,2:T(8,128)} copy(f32[128,32,6,2,64,1]{4,1,3,2,0,5:T(8,128)} %fusion.8) | data formatting | bytes 25165824 | tf_op jit(solution)/shard_map/sitkpv,pvn->sitkn/dot_general | solution.py:68
  299.3 19.0 %fusion = f32[64,64]{1,0:T(8,128)S(1)} fusion(f32[128]{0:T(128)S(1)} %copy-done.9, f32[128,32,6,2,64,1]{0,1,3,5,4,2:T(8,128)} %copy.42, f32[1,64,2,32]{1,3,2,0:T(8,128)S(1)} %copy-done.5, f32[1,64,2,32]{1,3,2,0:T(8,128)S(1)} %get-tuple-element.11), kind=kOutput, calls=%fused_computation.2 | convolution fusion | flops 2434797568 | bytes 12632576 | tf_op jit(solution)/shard_map/cxqi,sitkqy->tskcxy/dot_general | solution.py:70
  318.4 0.7 mul.233
  (45 shorter events, 1.1 us)
Async XLA Ops:
  0.0 1.0 copy-start
  8.0 178.6 %copy-start.3 = (bf16[256,2048]{1,0:T(8,128)(2,1)S(1)}, bf16[256,2048]{1,0:T(8,128)(2,1)}, u32[]{:S(2)}) copy-start(bf16[256,2048]{1,0:T(8,128)(2,1)} %param.8) | copy-start | bytes 3145732
  8.0 178.9 %copy-start.6 = (f32[2048]{0:T(1024)S(1)}, f32[2048]{0:T(1024)}, u32[]{:S(2)}) copy-start(f32[2048]{0:T(1024)} %param.9) | copy-start | bytes 24580
  181.3 6.5 %copy-start.8 = (s32[128]{0:T(128)S(1)}, s32[128]{0:T(128)}, u32[]{:S(2)}) copy-start(s32[128]{0:T(128)} %param.14) | copy-start | bytes 1540
  181.3 23.5 %collective-permute-start.3 = (bf16[2560,2816]{1,0:T(8,128)(2,1)}, bf16[2560,2816]{1,0:T(8,128)(2,1)}, u32[]{:S(2)}, u32[]{:S(2)}) collective-permute-start(bf16[2560,2816]{1,0:T(8,128)(2,1)} %bitcast.13), channel_id=1, source_target_pairs={{0,1},{1,0},{2,3},{3,2},{4,5},{5,4},{6,7},{7,6},{8,9},{9,8},{10,11... | collective-permute-start | bytes 43253768 | tf_op jit(solution)/shard_map/ppermute | solution.py:105
  183.0 51.0 %collective-permute-start = (bf16[2048,192]{0,1:T(8,128)(2,1)}, bf16[2048,192]{0,1:T(8,128)(2,1)}, u32[]{:S(2)}, u32[]{:S(2)}) collective-permute-start(bf16[2048,192]{0,1:T(8,128)(2,1)} %param.12), channel_id=1, source_target_pairs={{0,1},{1,0},{2,3},{3,2},{4,5},{5,4},{6,7},{7,6},{8,9},{9,8},{10,11... | collective-permute-start | bytes 2359304 | tf_op jit(solution)/shard_map/ppermute | solution.py:107
  183.0 51.0 %collective-permute-start.1 = (bf16[2048,192]{0,1:T(8,128)(2,1)}, bf16[2048,192]{0,1:T(8,128)(2,1)}, u32[]{:S(2)}, u32[]{:S(2)}) collective-permute-start(bf16[2048,192]{0,1:T(8,128)(2,1)} %param.12), channel_id=1, source_target_pairs={{0,2},{1,3},{2,0},{3,1},{4,6},{5,7},{6,4},{7,5},{8,10},{9,11},{10,... | collective-permute-start | bytes 2359304 | tf_op jit(solution)/shard_map/ppermute | solution.py:107
  185.5 48.6 %collective-permute-start.2 = (bf16[2048,192]{0,1:T(8,128)(2,1)}, bf16[2048,192]{0,1:T(8,128)(2,1)}, u32[]{:S(2)}, u32[]{:S(2)}) collective-permute-start(bf16[2048,192]{0,1:T(8,128)(2,1)} %param.12), channel_id=1, source_target_pairs={{0,3},{1,2},{2,1},{3,0},{4,7},{5,6},{6,5},{7,4},{8,11},{9,10},{10,... | collective-permute-start | bytes 2359304 | tf_op jit(solution)/shard_map/ppermute | solution.py:107
  187.8 1.4 copy-start.7
  223.6 10.5 %copy-start.4 = (bf16[256,2048]{1,0:T(8,128)(2,1)S(1)}, bf16[256,2048]{1,0:T(8,128)(2,1)}, u32[]{:S(2)}) copy-start(bf16[256,2048]{1,0:T(8,128)(2,1)} %param.8) | copy-start | bytes 3145732
  255.5 6.5 %copy-start.2 = (pred[128,32,128]{2,1,0:T(8,128)(4,1)S(1)}, pred[128,32,128]{2,1,0:T(8,128)(4,1)}, u32[]{:S(2)}) copy-start(pred[128,32,128]{2,1,0:T(8,128)(4,1)} %fusion.36) | copy-start | bytes 1572868
  276.6 22.7 %copy-start.5 = (f32[1,64,2,32]{1,3,2,0:T(8,128)S(1)}, f32[1,64,2,32]{1,3,2,0:T(8,128)}, u32[]{:S(2)}) copy-start(f32[1,64,2,32]{1,3,2,0:T(8,128)} %get-tuple-element.12) | copy-start | bytes 49156
  276.6 22.7 %copy-start.9 = (f32[128]{0:T(128)S(1)}, f32[128]{0:T(128)}, u32[]{:S(2)}) copy-start(f32[128]{0:T(128)} %param.15) | copy-start | bytes 1540
  299.3 19.8 %copy-start.1 = (bf16[88,2048]{1,0:T(8,128)(2,1)S(1)}, bf16[88,2048]{1,0:T(8,128)(2,1)}, u32[]{:S(2)}) copy-start(bf16[88,2048]{1,0:T(8,128)(2,1)} %param.11) | copy-start | bytes 1081348
